TPU v7x, 512 devices: a whole 4x4x16 slice. The times are simulated.
512 devices in a mesh: space: 16 (over z), chaos: 32 (over x, y, core).
Axes of the slice: x: 4, y: 4, z: 16, core: 2. Of those that a mesh axis runs over, the one named last changes fastest.
Arguments:
- forcing: float32 [960, 64, 128], P('chaos', 'space'), may hold values from -120 to 120
- mean_field: float32 [64, 128], P('space'), may hold values from 1 to 8
- modes: float32 [12, 64, 128], P(None, 'space'), may hold values from 0.02 to 0.05
- lengths: int32 [32], replicated, may hold values from 1 to 30, 455 in all
Outputs:
- solution: float32 [960, 64, 128], P('chaos', 'space')
- norms: float32 [3], replicated
Inputs may be any that keep to these rules, and one draw needn't show every extreme that they name: Group lengths are positive, sum to 455, and the largest is exactly 30.
All inputs are finite; a program needn't handle non-finite values.
Results may differ from a plain program's by a relative error of at most 0.0001.
Values sent between devices are 32-bit elements; how exact they have to be, the bound alone decides.
No kernel may reach another device: no remote copies, remote signals or barrier semaphores. Data moves between devices by JAX's collectives and lax.ppermute only.
A program may use at most 64 MiB of HBM per device.

v0:
```python
import math
import jax
import jax.numpy as jnp
import numpy as np
from jax import lax
from jax.sharding import PartitionSpec as P

M = 12
P_SIZE = 455
ITERS = 3
spectrum_low = 0.05
spectrum_high = 3.0


def padded(shard, sides, width):
    for axis, dim in sides:
        devices, length = (lax.axis_size(axis), shard.shape[dim])
        up = [(i, (i + 1) % devices) for i in range(devices - 1)]
        down = [(j, i) for i, j in up]
        last = lax.slice_in_dim(shard, length - width, length, axis=dim)
        first = lax.slice_in_dim(shard, 0, width, axis=dim)
        before = lax.ppermute(last, axis, up)
        after = lax.ppermute(first, axis, down)
        shard = jnp.concatenate([before, shard, after], axis=dim)
    return shard


def index_key(entry):
    return tuple((int(value) for value in entry))


def chaos_tables(terms):
    indices = [np.zeros(terms, dtype=np.int64)]
    for first in range(terms):
        entry = np.zeros(terms, dtype=np.int64)
        entry[first] += 1
        indices.append(entry)
    for first in range(terms):
        for second in range(first, terms):
            entry = np.zeros(terms, dtype=np.int64)
            entry[first] += 1
            entry[second] += 1
            indices.append(entry)
    for first in range(terms):
        for second in range(first, terms):
            for third in range(second, terms):
                entry = np.zeros(terms, dtype=np.int64)
                entry[first] += 1
                entry[second] += 1
                entry[third] += 1
                indices.append(entry)
    lookup = {}
    for number, entry in enumerate(indices):
        lookup[index_key(entry)] = number
    count = len(indices)
    upward = np.full((count, terms), count, dtype=np.int64)
    downward = np.full((count, terms), count, dtype=np.int64)
    up_coef = np.zeros((count, terms))
    down_coef = np.zeros((count, terms))
    for number, entry in enumerate(indices):
        for term in range(terms):
            if entry.sum() < 3:
                other = entry.copy()
                other[term] += 1
                upward[number, term] = lookup[index_key(other)]
                up_coef[number, term] = math.sqrt(entry[term] + 1)
            if entry[term] > 0:
                other = entry.copy()
                other[term] -= 1
                downward[number, term] = lookup[index_key(other)]
                down_coef[number, term] = math.sqrt(entry[term])
    return (
        upward.astype(np.int32),
        downward.astype(np.int32),
        up_coef.astype(np.float32),
        down_coef.astype(np.float32),
    )


def shifted(values, toward):
    blank = jnp.zeros_like(values[..., :1])
    if toward > 0:
        return jnp.concatenate([values[..., 1:], blank], axis=-1)
    return jnp.concatenate([blank, values[..., :-1]], axis=-1)


def stiffness(field_pad, tile_pad):
    center_field = field_pad[..., 1:-1, :]
    center_tile = tile_pad[..., 1:-1, :]
    result = 0.5 * (center_field + field_pad[..., :-2, :]) * (center_tile - tile_pad[..., :-2, :])
    result = result + 0.5 * (center_field + field_pad[..., 2:, :]) * (
        center_tile - tile_pad[..., 2:, :]
    )
    for toward in (1, -1):
        result = result + 0.5 * (center_field + shifted(center_field, toward)) * (
            center_tile - shifted(center_tile, toward)
        )
    return result


def diagonal_of(field_pad):
    center_field = field_pad[..., 1:-1, :]
    result = 0.5 * (center_field + field_pad[..., :-2, :])
    result = result + 0.5 * (center_field + field_pad[..., 2:, :])
    for toward in (1, -1):
        result = result + 0.5 * (center_field + shifted(center_field, toward))
    return result


def local(forcing, mean_field, modes, lengths):
    slot_cap, tile_rows, tile_cols = forcing.shape
    groups = lax.axis_size("chaos")
    slot_count = slot_cap * groups
    my_group = lax.axis_index("chaos")
    upward, downward, up_coef, down_coef = chaos_tables(M)
    group_ends = jnp.cumsum(lengths).astype(jnp.int32)
    group_starts = (group_ends - lengths).astype(jnp.int32)
    slot_index = jnp.arange(slot_cap, dtype=jnp.int32)
    live_grid = slot_index[None, :] < lengths[:, None]
    ids_grid = jnp.where(live_grid, group_starts[:, None] + slot_index[None, :], -1).astype(
        jnp.int32
    )
    all_ids = ids_grid.reshape(slot_count)
    mine = lax.dynamic_slice_in_dim(ids_grid, my_group, 1, 0)[0]
    my_live = mine >= 0
    safe_ids = jnp.clip(mine, 0, P_SIZE - 1)
    up_rows = jnp.take(jnp.asarray(upward), safe_ids, axis=0)
    down_rows = jnp.take(jnp.asarray(downward), safe_ids, axis=0)
    live_float = my_live.astype(jnp.float32)
    up_weight = jnp.take(jnp.asarray(up_coef), safe_ids, axis=0) * live_float[:, None]
    down_weight = jnp.take(jnp.asarray(down_coef), safe_ids, axis=0) * live_float[:, None]
    coupling = jnp.where(
        up_rows.T[:, :, None] == all_ids[None, None, :], up_weight.T[:, :, None], 0.0
    )
    coupling = coupling + jnp.where(
        down_rows.T[:, :, None] == all_ids[None, None, :], down_weight.T[:, :, None], 0.0
    )
    coupling = coupling.reshape(M * slot_cap, slot_count)
    raw_fields = jnp.concatenate([mean_field[None], modes], axis=0)
    raw_pad = padded(raw_fields, (("space", 1),), 1)
    fields_pad = jnp.concatenate([raw_pad[:1], raw_pad[:1] * raw_pad[1:]], axis=0)
    diagonal = diagonal_of(raw_pad[0])
    theta = (spectrum_high + spectrum_low) / 2.0
    delta = (spectrum_high - spectrum_low) / 2.0
    sigma = theta / delta
    rho = 1.0 / sigma
    residual = forcing * live_float[:, None, None]
    solution = jnp.zeros_like(residual)
    direction = residual / diagonal / theta
    norm_list = []
    for sweep_index in range(ITERS):
        solution = solution + direction
        initial = jnp.zeros((M * slot_cap, tile_rows * tile_cols), jnp.float32)
        piece = jax.tree.map(
            lambda part: lax.all_gather(part, "chaos", axis=0, tiled=True), direction
        )
        count = piece.shape[0]
        block = lax.slice_in_dim(coupling, 0, count, axis=1)
        mixed = initial + jnp.dot(
            block,
            piece.reshape(count, -1),
            precision=lax.Precision.HIGHEST,
            preferred_element_type=jnp.float32,
        )
        mixed = mixed.reshape(M, slot_cap, tile_rows, tile_cols)
        stacked = jnp.concatenate([direction[None], mixed], axis=0)
        stacked = padded(stacked, (("space", 2),), 1)
        residual = residual - jnp.sum(stiffness(fields_pad[:, None], stacked), axis=0)
        partial_value = jnp.sum(residual * residual)
        norm_list.append(jnp.sqrt(lax.psum(partial_value, ("space", "chaos"))))
        if sweep_index + 1 < ITERS:
            rho_new = 1.0 / (2.0 * sigma - rho)
            direction = rho_new * rho * direction + 2.0 * rho_new / delta * (residual / diagonal)
            rho = rho_new
    norms = jnp.stack(norm_list)
    return (solution, norms)


def solution(mesh):
    in_specs = (P("chaos", "space", None), P("space", None), P(None, "space", None), P())
    out_specs = (P("chaos", "space", None), P())
    return jax.shard_map(local, mesh=mesh, in_specs=in_specs, out_specs=out_specs, check_vma=False)
```

profile of v0, /device:TPU:1, one launch (start us, length us, event | category | flops | bytes accessed | tf_op | source)
XLA Modules:
  0.0 371.4 jit_solution(11172319493625132148)
XLA Ops:
  7.2 0.8 pad_maximum_fusion.19
  8.0 4.4 %collective-permute-start = (f32[13,1,128]{2,1,0:T(1,128)S(1)}, f32[13,1,128]{2,1,0:T(1,128)S(1)}, u32[]{:S(2)}, u32[]{:S(2)}) collective-permute-start(f32[13,1,128]{2,1,0:T(1,128)S(1)} %get-tuple-element.41), channel_id=1, source_target_pairs={{0,32},{32,64},{64,96},{96,128},{128,160},{160,192},{192,224},{224... | collective-permute-start | bytes 19976 | tf_op jit(solution)/shard_map/ppermute | solution.py:22
  12.4 1.3 collective-permute-start.1
  13.7 0.8 fusion.94
  14.5 0.7 copy.30
  16.1 0.7 add_select_fusion
  17.0 0.9 fusion.83
  17.8 0.9 fusion.91
  19.6 1.5 gather_fusion.3
  21.2 1.5 gather_fusion.2
  22.7 1.5 gather_fusion.1
  24.4 1.5 gather_fusion
  26.9 0.8 fusion.71
  27.8 57.6 %all-gather.4.cloned.1.call-done = f32[960,4,128]{2,1,0:T(4,128)} async-done(((f32[30,4,128]{2,1,0:T(4,128)}), f32[960,4,128]{2,1,0:T(4,128)}) %all-gather.4.cloned.1.call-update) | async-done | bytes 1966096 | tf_op jit(solution)/shard_map/all_gather | solution.py:155
  85.3 4.5 %fusion.4 = f32[12,30,4,128]{3,1,2,0:T(8,128)S(1)} fusion(f32[12,30]{1,0:T(8,128)S(1)} %copy.35, s32[12,30]{1,0:T(8,128)S(1)} %copy.34, f32[12,30]{1,0:T(8,128)S(1)} %copy.33, s32[960]{0:T(1024)S(1)} %select_n.56, s32[12,30]{1,0:T(8,128)S(1)} %copy.32, f32[120,8,4,128]{3,2,1,0:T(4,128)} %bitcast.120), kind=kOutput, calls=%fused_computation.29 | convolution fusion | flops 2125094400 | bytes 2712960 | tf_op jit(solution)/shard_map/dot_general | solution.py:159
  89.9 3.2 collective-permute-start.2
  93.1 1.3 collective-permute-start.3
  94.8 2.6 collective-permute-done.2
  97.4 3.8 %collective-permute-done.3 = f32[13,30,1,128]{3,1,2,0:T(8,128)S(1)} collective-permute-done((f32[13,30,1,128]{3,1,2,0:T(8,128)S(1)}, f32[13,30,1,128]{3,1,2,0:T(8,128)S(1)}, u32[]{:S(2)}, u32[]{:S(2)}) %collective-permute-start.3) | collective-permute-done | bytes 199712 | tf_op jit(solution)/shard_map/ppermute | solution.py:23
  102.9 59.5 %all-gather.6.cloned.1.call-done = f32[960,4,128]{2,1,0:T(4,128)} async-done(((f32[30,4,128]{2,1,0:T(4,128)}), f32[960,4,128]{2,1,0:T(4,128)}) %all-gather.6.cloned.1.call-update) | async-done | bytes 1966096 | tf_op jit(solution)/shard_map/all_gather | solution.py:155
  162.4 4.5 %fusion.2 = f32[12,30,4,128]{3,1,2,0:T(8,128)S(1)} fusion(f32[12,30]{1,0:T(8,128)S(1)} %copy.35, s32[12,30]{1,0:T(8,128)S(1)} %copy.34, f32[12,30]{1,0:T(8,128)S(1)} %copy.33, s32[960]{0:T(1024)S(1)} %select_n.56, s32[12,30]{1,0:T(8,128)S(1)} %copy.32, f32[120,8,4,128]{3,2,1,0:T(4,128)} %bitcast.122), kind=kOutput, calls=%fused_computation.26 | convolution fusion | flops 2125094400 | bytes 2712960 | tf_op jit(solution)/shard_map/dot_general | solution.py:159
  167.0 3.2 collective-permute-start.4
  170.2 1.3 collective-permute-start.5
  171.8 2.7 collective-permute-done.4
  174.4 3.8 %collective-permute-done.5 = f32[13,30,1,128]{3,1,2,0:T(8,128)S(1)} collective-permute-done((f32[13,30,1,128]{3,1,2,0:T(8,128)S(1)}, f32[13,30,1,128]{3,1,2,0:T(8,128)S(1)}, u32[]{:S(2)}, u32[]{:S(2)}) %collective-permute-start.5) | collective-permute-done | bytes 199712 | tf_op jit(solution)/shard_map/ppermute | solution.py:23
  180.3 59.6 %all-gather.8.cloned.1.call-done = f32[960,4,128]{2,1,0:T(4,128)} async-done(((f32[30,4,128]{2,1,0:T(4,128)}), f32[960,4,128]{2,1,0:T(4,128)}) %all-gather.8.cloned.1.call-update) | async-done | bytes 1966096 | tf_op jit(solution)/shard_map/all_gather | solution.py:155
  239.9 4.5 %fusion = f32[12,30,4,128]{3,1,2,0:T(8,128)S(1)} fusion(f32[12,30]{1,0:T(8,128)S(1)} %copy.35, s32[12,30]{1,0:T(8,128)S(1)} %copy.34, f32[12,30]{1,0:T(8,128)S(1)} %copy.33, s32[960]{0:T(1024)S(1)} %select_n.56, s32[12,30]{1,0:T(8,128)S(1)} %copy.32, f32[120,8,4,128]{3,2,1,0:T(4,128)} %bitcast.121), kind=kOutput, calls=%fused_computation.23 | convolution fusion | flops 2125094400 | bytes 2712960 | tf_op jit(solution)/shard_map/dot_general | solution.py:159
  244.4 3.2 collective-permute-start.6
  247.6 1.3 collective-permute-start.7
  249.9 2.0 collective-permute-done.6
  251.9 3.8 %collective-permute-done.7 = f32[13,30,1,128]{3,1,2,0:T(8,128)S(1)} collective-permute-done((f32[13,30,1,128]{3,1,2,0:T(8,128)S(1)}, f32[13,30,1,128]{3,1,2,0:T(8,128)S(1)}, u32[]{:S(2)}, u32[]{:S(2)}) %collective-permute-start.7) | collective-permute-done | bytes 199712 | tf_op jit(solution)/shard_map/ppermute | solution.py:23
  257.1 105.2 %all-reduce.10 = (f32[]{:T(128)}, f32[]{:T(128)}, f32[]{:T(128)}) all-reduce(f32[]{:T(128)} %get-tuple-element.11, f32[]{:T(128)} %get-tuple-element.10, f32[]{:T(128)} %get-tuple-element.32), channel_id=1, replica_groups=mesh['space'=16,'chaos'=32] {'space','chaos'}, use_global_device_ids=true, to_apply=%region_9.12 | all-reduce | flops 3 | bytes 24 | tf_op jit(solution)/shard_map/psum | solution.py:170
  (44 shorter events, 10.4 us)
Async XLA Ops:
  7.2 78.2 %all-gather.4.cloned.1.call-start = ((), (), s32[]{:S(2)}) async-start(), calls=%async_computation | async-start | bytes 2027520 | tf_op jit(solution)/shard_map/all_gather | solution.py:155
  8.0 8.8 %collective-permute-start = (f32[13,1,128]{2,1,0:T(1,128)S(1)}, f32[13,1,128]{2,1,0:T(1,128)S(1)}, u32[]{:S(2)}, u32[]{:S(2)}) collective-permute-start(f32[13,1,128]{2,1,0:T(1,128)S(1)} %get-tuple-element.41), channel_id=1, source_target_pairs={{0,32},{32,64},{64,96},{96,128},{128,160},{160,192},{192,224},{224... | collective-permute-start | bytes 19976 | tf_op jit(solution)/shard_map/ppermute | solution.py:22
  12.4 4.6 %collective-permute-start.1 = (f32[13,1,128]{2,1,0:T(1,128)S(1)}, f32[13,1,128]{2,1,0:T(1,128)S(1)}, u32[]{:S(2)}, u32[]{:S(2)}) collective-permute-start(f32[13,1,128]{2,1,0:T(1,128)S(1)} %get-tuple-element.42), channel_id=1, source_target_pairs={{32,0},{64,32},{96,64},{128,96},{160,128},{192,160},{224,192},{256... | collective-permute-start | bytes 19976 | tf_op jit(solution)/shard_map/ppermute | solution.py:23
  19.5 143.0 %all-gather.6.cloned.1.call-start = ((), (), s32[]{:S(2)}) async-start(), calls=%async_computation.1 | async-start | bytes 2027520 | tf_op jit(solution)/shard_map/all_gather | solution.py:155
  89.9 7.5 %collective-permute-start.2 = (f32[13,30,1,128]{3,1,2,0:T(8,128)S(1)}, f32[13,30,1,128]{3,1,2,0:T(8,128)S(1)}, u32[]{:S(2)}, u32[]{:S(2)}) collective-permute-start(f32[13,30,1,128]{3,1,2,0:T(8,128)S(1)} %get-tuple-element.30), channel_id=1, source_target_pairs={{0,32},{32,64},{64,96},{96,128},{128,160},{160,192},{192,224},{224... | collective-permute-start | bytes 599048 | tf_op jit(solution)/shard_map/ppermute | solution.py:22
  93.1 8.1 %collective-permute-start.3 = (f32[13,30,1,128]{3,1,2,0:T(8,128)S(1)}, f32[13,30,1,128]{3,1,2,0:T(8,128)S(1)}, u32[]{:S(2)}, u32[]{:S(2)}) collective-permute-start(f32[13,30,1,128]{3,1,2,0:T(8,128)S(1)} %get-tuple-element.31), channel_id=1, source_target_pairs={{32,0},{64,32},{96,64},{128,96},{160,128},{192,160},{224,192},{256... | collective-permute-start | bytes 599048 | tf_op jit(solution)/shard_map/ppermute | solution.py:23
  101.2 0.8 copy-start
  102.8 137.1 %all-gather.8.cloned.1.call-start = ((), (), s32[]{:S(2)}) async-start(), calls=%async_computation.2 | async-start | bytes 2027520 | tf_op jit(solution)/shard_map/all_gather | solution.py:155
  167.0 7.5 %collective-permute-start.4 = (f32[13,30,1,128]{3,1,2,0:T(8,128)S(1)}, f32[13,30,1,128]{3,1,2,0:T(8,128)S(1)}, u32[]{:S(2)}, u32[]{:S(2)}) collective-permute-start(f32[13,30,1,128]{3,1,2,0:T(8,128)S(1)} %get-tuple-element.26), channel_id=1, source_target_pairs={{0,32},{32,64},{64,96},{96,128},{128,160},{160,192},{192,224},{224... | collective-permute-start | bytes 599048 | tf_op jit(solution)/shard_map/ppermute | solution.py:22
  170.2 8.1 %collective-permute-start.5 = (f32[13,30,1,128]{3,1,2,0:T(8,128)S(1)}, f32[13,30,1,128]{3,1,2,0:T(8,128)S(1)}, u32[]{:S(2)}, u32[]{:S(2)}) collective-permute-start(f32[13,30,1,128]{3,1,2,0:T(8,128)S(1)} %get-tuple-element.27), channel_id=1, source_target_pairs={{32,0},{64,32},{96,64},{128,96},{160,128},{192,160},{224,192},{256... | collective-permute-start | bytes 599048 | tf_op jit(solution)/shard_map/ppermute | solution.py:23
  244.4 7.5 %collective-permute-start.6 = (f32[13,30,1,128]{3,1,2,0:T(8,128)S(1)}, f32[13,30,1,128]{3,1,2,0:T(8,128)S(1)}, u32[]{:S(2)}, u32[]{:S(2)}) collective-permute-start(f32[13,30,1,128]{3,1,2,0:T(8,128)S(1)} %get-tuple-element.22), channel_id=1, source_target_pairs={{0,32},{32,64},{64,96},{96,128},{128,160},{160,192},{192,224},{224... | collective-permute-start | bytes 599048 | tf_op jit(solution)/shard_map/ppermute | solution.py:22
  247.6 8.1 %collective-permute-start.7 = (f32[13,30,1,128]{3,1,2,0:T(8,128)S(1)}, f32[13,30,1,128]{3,1,2,0:T(8,128)S(1)}, u32[]{:S(2)}, u32[]{:S(2)}) collective-permute-start(f32[13,30,1,128]{3,1,2,0:T(8,128)S(1)} %get-tuple-element.23), channel_id=1, source_target_pairs={{32,0},{64,32},{96,64},{128,96},{160,128},{192,160},{224,192},{256... | collective-permute-start | bytes 599048 | tf_op jit(solution)/shard_map/ppermute | solution.py:23
Sparse Core Ops, SparseCore 0:
  19.6 65.7 all-gather.3
  102.9 59.4 all-gather.5
  180.4 59.4 all-gather.7
where the time goes:
time: 372 us; the launch traced here: 371 us
  waiting for transfers between devices  196 us (53%)
  blocking collectives  105 us (28%)
  starting transfers between devices  19.2 us (5%)
  between operations  16 us (4%)
  matrix products  13.5 us (4%)
  local copies, waits for them, and re-layouts  11 us (3%)
  other arithmetic  10.8 us (3%)
    all_gather x3, waiting for transfers between devices, local(): lax.all_gather(part, 'chaos', axis=0, tiled=True)  177 us
    psum x1, blocking collectives, local(): norm_list.append(jnp.sqrt(lax.psum(partial_value, ('space', 'chaos'))))  105 us
    ppermute x4, starting transfers between devices, padded(): before = lax.ppermute(last, axis, up)  13.9 us
    dot_general x3, matrix products, local(): jnp.dot(block, piece.reshape(count, -1), precision=lax.Precision.HIGHEST,...  13.5 us
    ppermute x4, waiting for transfers between devices, padded(): after = lax.ppermute(first, axis, down)  11.6 us
  transfers between devices with their start and end apart: 11, of which 10 were waited for; matrix products, arithmetic and copies ran while one was open for 4% of the time, Pallas kernels for 0%

commit v1 on v0

--- a/solution.py
+++ b/solution.py
@@ -152,7 +152,10 @@
         solution = solution + direction
         initial = jnp.zeros((M * slot_cap, tile_rows * tile_cols), jnp.float32)
         piece = jax.tree.map(
-            lambda part: lax.all_gather(part, "chaos", axis=0, tiled=True), direction
+            lambda part: jnp.concatenate(
+                lax.all_to_all(jnp.stack(lax.axis_size("chaos") * [part]), "chaos", 0, 0), 0
+            ),
+            direction,
         )
         count = piece.shape[0]
         block = lax.slice_in_dim(coupling, 0, count, axis=1)

time: 372 us -> 272 us (0.73)
  waiting for transfers between devices: 196 us -> 44.4 us
  blocking collectives: 105 us -> 167 us
  between operations: 16 us -> 2.96 us
  starting transfers between devices: 19.2 us -> 31.5 us
  matrix products: 13.5 us -> 8.87 us
    all_gather x3 -> x0, waiting for transfers between devices: 177 us -> none  [local(): lax.all_gather(part, 'chaos', axis=0, tiled=True)]
    all_to_all x0 -> x2, blocking collectives: none -> 62.5 us  [local(): lax.all_to_all(jnp.stack(lax.axis_size('chaos') * [part]), 'chaos', 0, 0)]
    all_to_all x0 -> x1, waiting for transfers between devices: none -> 23.8 us  [local(): lax.all_to_all(jnp.stack(lax.axis_size('chaos') * [part]), 'chaos', 0, 0)]
    all_to_all x0 -> x1, starting transfers between devices: none -> 9.14 us  [local(): lax.all_to_all(jnp.stack(lax.axis_size('chaos') * [part]), 'chaos', 0, 0)]
    dot_general x3, matrix products: 13.5 us -> 8.87 us  [local(): jnp.dot(block, piece.reshape(count, -1), precision=lax.Precision.HIGHEST,...]
  transfers between devices with their start and end apart: 11 -> 9, of which waited for: 10 -> 8; matrix products, arithmetic and copies ran while one was open for 4% -> 3% of each run, Pallas kernels for 0% -> 0%
where the time goes in v1:
time: 272 us; the launch traced here: 271 us
  blocking collectives  167 us (61%)
  waiting for transfers between devices  44.4 us (16%)
  starting transfers between devices  31.5 us (12%)
  other arithmetic  9.34 us (3%)
  matrix products  8.87 us (3%)
  local copies, waits for them, and re-layouts  7.51 us (3%)
  between operations  2.96 us (1%)
    psum x1, blocking collectives, local(): norm_list.append(jnp.sqrt(lax.psum(partial_value, ('space', 'chaos'))))  104 us
    all_to_all x2, blocking collectives, local(): lax.all_to_all(jnp.stack(lax.axis_size('chaos') * [part]), 'chaos', 0, 0)  62.5 us
    all_to_all x1, waiting for transfers between devices, local(): lax.all_to_all(jnp.stack(lax.axis_size('chaos') * [part]), 'chaos', 0, 0)  23.8 us
    ppermute x4, starting transfers between devices, padded(): before = lax.ppermute(last, axis, up)  17.2 us
    ppermute x4, waiting for transfers between devices, padded(): after = lax.ppermute(first, axis, down)  13.2 us
    all_to_all x1, starting transfers between devices, local(): lax.all_to_all(jnp.stack(lax.axis_size('chaos') * [part]), 'chaos', 0, 0)  9.14 us
    dot_general x3, matrix products, local(): jnp.dot(block, piece.reshape(count, -1), precision=lax.Precision.HIGHEST,...  8.87 us
    ppermute x4, waiting for transfers between devices, padded(): before = lax.ppermute(last, axis, up)  7.36 us
  transfers between devices with their start and end apart: 9, of which 8 were waited for; matrix products, arithmetic and copies ran while one was open for 3% of the time, Pallas kernels for 0%

profile of v1, /device:TPU:1, one launch (start us, length us, event | category | flops | bytes accessed | tf_op | source)
XLA Modules:
  0.0 271.5 jit_solution(11982641661533638281)
XLA Ops:
  0.6 0.8 pad_maximum_fusion.19
  1.5 4.4 %collective-permute-start = (f32[13,1,128]{2,1,0:T(1,128)S(1)}, f32[13,1,128]{2,1,0:T(1,128)S(1)}, u32[]{:S(2)}, u32[]{:S(2)}) collective-permute-start(f32[13,1,128]{2,1,0:T(1,128)S(1)} %get-tuple-element.39), channel_id=1, source_target_pairs={{0,32},{32,64},{64,96},{96,128},{128,160},{160,192},{192,224},{224... | collective-permute-start | bytes 19976 | tf_op jit(solution)/shard_map/ppermute | solution.py:22
  5.8 1.3 collective-permute-start.1
  7.1 0.8 fusion.94
  8.0 0.7 copy.20
  9.5 0.7 add_select_fusion
  10.4 0.9 fusion.83
  11.3 0.9 fusion.91
  12.2 1.6 stack.14
  13.8 9.1 %all-to-all-start = ((f32[32,30,4,128]{3,2,1,0:T(4,128)}), f32[32,30,4,128]{3,2,1,0:T(4,128)S(1)}, u32[]{:S(2)}, u32[]{:S(2)}) async-start(f32[32,30,4,128]{3,2,1,0:T(4,128)} %stack.14), calls=%async_computation | async-start | bytes 3932160 | tf_op jit(solution)/shard_map/all_to_all | solution.py:156
  26.1 23.8 %all-to-all-done = f32[32,30,4,128]{3,2,1,0:T(4,128)S(1)} async-done(((f32[32,30,4,128]{3,2,1,0:T(4,128)}), f32[32,30,4,128]{3,2,1,0:T(4,128)S(1)}, u32[]{:S(2)}, u32[]{:S(2)}) %all-to-all-start) | async-done | bytes 1966112 | tf_op jit(solution)/shard_map/all_to_all | solution.py:156
  49.9 3.0 %fusion.4 = f32[12,30,4,128]{3,1,2,0:T(8,128)S(1)} fusion(f32[12,30]{1,0:T(8,128)S(1)} %copy.25, s32[12,30]{1,0:T(8,128)S(1)} %copy.24, f32[12,30]{1,0:T(8,128)S(1)} %copy.23, s32[960]{0:T(1024)S(1)} %select_n.56, s32[12,30]{1,0:T(8,128)S(1)} %copy.22, f32[120,8,4,128]{3,2,1,0:T(4,128)S(1)} %bitcast.114), kind=kOutput, calls=%fused_computation.29 | convolution fusion | flops 2125094400 | bytes 2712960 | tf_op jit(solution)/shard_map/dot_general | solution.py:162
  52.9 3.6 %collective-permute-start.2 = (f32[13,30,1,128]{3,1,2,0:T(8,128)S(1)}, f32[13,30,1,128]{3,1,2,0:T(8,128)S(1)}, u32[]{:S(2)}, u32[]{:S(2)}) collective-permute-start(f32[13,30,1,128]{3,1,2,0:T(8,128)S(1)} %get-tuple-element.28), channel_id=1, source_target_pairs={{0,32},{32,64},{64,96},{96,128},{128,160},{160,192},{192,224},{224... | collective-permute-start | bytes 599048 | tf_op jit(solution)/shard_map/ppermute | solution.py:22
  56.5 1.3 collective-permute-start.3
  58.2 2.1 collective-permute-done.2
  60.3 5.4 %collective-permute-done.3 = f32[13,30,1,128]{3,1,2,0:T(8,128)S(1)} collective-permute-done((f32[13,30,1,128]{3,1,2,0:T(8,128)S(1)}, f32[13,30,1,128]{3,1,2,0:T(8,128)S(1)}, u32[]{:S(2)}, u32[]{:S(2)}) %collective-permute-start.3) | collective-permute-done | bytes 199712 | tf_op jit(solution)/shard_map/ppermute | solution.py:23
  66.9 31.3 %all_to_all.15 = f32[32,30,4,128]{3,2,1,0:T(4,128)S(1)} all-to-all(f32[32,30,4,128]{3,2,1,0:T(4,128)S(1)} %stack.15), channel_id=1, replica_groups=mesh['space'=16,'chaos'=32] {'chaos'}, dimensions={0} | all-to-all | bytes 3932160 | tf_op jit(solution)/shard_map/all_to_all | solution.py:156
  98.3 3.0 %fusion.2 = f32[12,30,4,128]{3,1,2,0:T(8,128)S(1)} fusion(f32[12,30]{1,0:T(8,128)S(1)} %copy.25, s32[12,30]{1,0:T(8,128)S(1)} %copy.24, f32[12,30]{1,0:T(8,128)S(1)} %copy.23, s32[960]{0:T(1024)S(1)} %select_n.56, s32[12,30]{1,0:T(8,128)S(1)} %copy.22, f32[120,8,4,128]{3,2,1,0:T(4,128)S(1)} %bitcast.116), kind=kOutput, calls=%fused_computation.26 | convolution fusion | flops 2125094400 | bytes 2712960 | tf_op jit(solution)/shard_map/dot_general | solution.py:162
  101.3 4.9 %collective-permute-start.4 = (f32[13,30,1,128]{3,1,2,0:T(8,128)S(1)}, f32[13,30,1,128]{3,1,2,0:T(8,128)S(1)}, u32[]{:S(2)}, u32[]{:S(2)}) collective-permute-start(f32[13,30,1,128]{3,1,2,0:T(8,128)S(1)} %get-tuple-element.24), channel_id=1, source_target_pairs={{0,32},{32,64},{64,96},{96,128},{128,160},{160,192},{192,224},{224... | collective-permute-start | bytes 599048 | tf_op jit(solution)/shard_map/ppermute | solution.py:22
  106.2 1.3 collective-permute-start.5
  107.8 3.0 %collective-permute-done.4 = f32[13,30,1,128]{3,1,2,0:T(8,128)S(1)} collective-permute-done((f32[13,30,1,128]{3,1,2,0:T(8,128)S(1)}, f32[13,30,1,128]{3,1,2,0:T(8,128)S(1)}, u32[]{:S(2)}, u32[]{:S(2)}) %collective-permute-start.4) | collective-permute-done | bytes 199712 | tf_op jit(solution)/shard_map/ppermute | solution.py:22
  110.7 3.8 %collective-permute-done.5 = f32[13,30,1,128]{3,1,2,0:T(8,128)S(1)} collective-permute-done((f32[13,30,1,128]{3,1,2,0:T(8,128)S(1)}, f32[13,30,1,128]{3,1,2,0:T(8,128)S(1)}, u32[]{:S(2)}, u32[]{:S(2)}) %collective-permute-start.5) | collective-permute-done | bytes 199712 | tf_op jit(solution)/shard_map/ppermute | solution.py:23
  115.2 0.7 add_add_fusion
  116.2 31.2 %all_to_all.16 = f32[32,30,4,128]{3,2,1,0:T(4,128)S(1)} all-to-all(f32[32,30,4,128]{3,2,1,0:T(4,128)S(1)} %stack.18), channel_id=1, replica_groups=mesh['space'=16,'chaos'=32] {'chaos'}, dimensions={0} | all-to-all | bytes 3932160 | tf_op jit(solution)/shard_map/all_to_all | solution.py:156
  147.4 3.0 %fusion = f32[12,30,4,128]{3,1,2,0:T(8,128)S(1)} fusion(f32[12,30]{1,0:T(8,128)S(1)} %copy.25, s32[12,30]{1,0:T(8,128)S(1)} %copy.24, f32[12,30]{1,0:T(8,128)S(1)} %copy.23, s32[960]{0:T(1024)S(1)} %select_n.56, s32[12,30]{1,0:T(8,128)S(1)} %copy.22, f32[120,8,4,128]{3,2,1,0:T(4,128)S(1)} %bitcast.115), kind=kOutput, calls=%fused_computation.23 | convolution fusion | flops 2125094400 | bytes 2712960 | tf_op jit(solution)/shard_map/dot_general | solution.py:162
  150.4 4.4 %collective-permute-start.6 = (f32[13,30,1,128]{3,1,2,0:T(8,128)S(1)}, f32[13,30,1,128]{3,1,2,0:T(8,128)S(1)}, u32[]{:S(2)}, u32[]{:S(2)}) collective-permute-start(f32[13,30,1,128]{3,1,2,0:T(8,128)S(1)} %get-tuple-element.20), channel_id=1, source_target_pairs={{0,32},{32,64},{64,96},{96,128},{128,160},{160,192},{192,224},{224... | collective-permute-start | bytes 599048 | tf_op jit(solution)/shard_map/ppermute | solution.py:22
  154.8 1.3 collective-permute-start.7
  156.1 0.7 copy.32
  157.1 2.3 collective-permute-done.6
  159.4 3.8 %collective-permute-done.7 = f32[13,30,1,128]{3,1,2,0:T(8,128)S(1)} collective-permute-done((f32[13,30,1,128]{3,1,2,0:T(8,128)S(1)}, f32[13,30,1,128]{3,1,2,0:T(8,128)S(1)}, u32[]{:S(2)}, u32[]{:S(2)}) %collective-permute-start.7) | collective-permute-done | bytes 199712 | tf_op jit(solution)/shard_map/ppermute | solution.py:23
  163.9 0.7 multiply_reduce_fusion.1
  164.5 104.4 %all-reduce.10 = (f32[]{:T(128)}, f32[]{:T(128)}, f32[]{:T(128)}) all-reduce(f32[]{:T(128)} %get-tuple-element.9, f32[]{:T(128)} %get-tuple-element.8, f32[]{:T(128)} %get-tuple-element.30), channel_id=1, replica_groups=mesh['space'=16,'chaos'=32] {'space','chaos'}, use_global_device_ids=true, to_apply=%region_9.12 | all-reduce | flops 3 | bytes 24 | tf_op jit(solution)/shard_map/psum | solution.py:173
  (54 shorter events, 8.5 us)
Async XLA Ops:
  1.5 8.8 %collective-permute-start = (f32[13,1,128]{2,1,0:T(1,128)S(1)}, f32[13,1,128]{2,1,0:T(1,128)S(1)}, u32[]{:S(2)}, u32[]{:S(2)}) collective-permute-start(f32[13,1,128]{2,1,0:T(1,128)S(1)} %get-tuple-element.39), channel_id=1, source_target_pairs={{0,32},{32,64},{64,96},{96,128},{128,160},{160,192},{192,224},{224... | collective-permute-start | bytes 19976 | tf_op jit(solution)/shard_map/ppermute | solution.py:22
  5.8 4.6 %collective-permute-start.1 = (f32[13,1,128]{2,1,0:T(1,128)S(1)}, f32[13,1,128]{2,1,0:T(1,128)S(1)}, u32[]{:S(2)}, u32[]{:S(2)}) collective-permute-start(f32[13,1,128]{2,1,0:T(1,128)S(1)} %get-tuple-element.40), channel_id=1, source_target_pairs={{32,0},{64,32},{96,64},{128,96},{160,128},{192,160},{224,192},{256... | collective-permute-start | bytes 19976 | tf_op jit(solution)/shard_map/ppermute | solution.py:23
  13.8 9.3 %copy-start.6 = (f32[455,12]{1,0:T(8,128)S(1)}, f32[455,12]{1,0:T(8,128)}, u32[]{:S(2)}) copy-start(f32[455,12]{1,0:T(8,128)} %constant.22.clone2.1) | copy-start | bytes 65524
  13.8 9.9 %copy-start.5 = (s32[455,12]{1,0:T(8,128)S(1)}, s32[455,12]{1,0:T(8,128)}, u32[]{:S(2)}) copy-start(s32[455,12]{1,0:T(8,128)} %constant.16.clone2.1) | copy-start | bytes 65524
  13.8 10.5 %copy-start.4 = (f32[455,12]{1,0:T(8,128)S(1)}, f32[455,12]{1,0:T(8,128)}, u32[]{:S(2)}) copy-start(f32[455,12]{1,0:T(8,128)} %constant.21.clone2.1) | copy-start | bytes 65524
  13.8 11.3 %copy-start.3 = (s32[455,12]{1,0:T(8,128)S(1)}, s32[455,12]{1,0:T(8,128)}, u32[]{:S(2)}) copy-start(s32[455,12]{1,0:T(8,128)} %constant.15.clone2.1) | copy-start | bytes 65524
  13.8 12.2 %copy-start.1 = (f32[12,4,128]{2,1,0:T(4,128)S(1)}, f32[12,4,128]{2,1,0:T(4,128)}, u32[]{:S(2)}) copy-start(f32[12,4,128]{2,1,0:T(4,128)} %param.14) | copy-start | bytes 73732
  13.8 12.1 %copy-start.2 = (f32[4,128]{1,0:T(4,128)S(1)}, f32[4,128]{1,0:T(4,128)}, u32[]{:S(2)}) copy-start(f32[4,128]{1,0:T(4,128)} %param.13) | copy-start | bytes 6148
  13.8 36.1 %all-to-all-start = ((f32[32,30,4,128]{3,2,1,0:T(4,128)}), f32[32,30,4,128]{3,2,1,0:T(4,128)S(1)}, u32[]{:S(2)}, u32[]{:S(2)}) async-start(f32[32,30,4,128]{3,2,1,0:T(4,128)} %stack.14), calls=%async_computation | async-start | bytes 3932160 | tf_op jit(solution)/shard_map/all_to_all | solution.py:156
  52.9 7.4 %collective-permute-start.2 = (f32[13,30,1,128]{3,1,2,0:T(8,128)S(1)}, f32[13,30,1,128]{3,1,2,0:T(8,128)S(1)}, u32[]{:S(2)}, u32[]{:S(2)}) collective-permute-start(f32[13,30,1,128]{3,1,2,0:T(8,128)S(1)} %get-tuple-element.28), channel_id=1, source_target_pairs={{0,32},{32,64},{64,96},{96,128},{128,160},{160,192},{192,224},{224... | collective-permute-start | bytes 599048 | tf_op jit(solution)/shard_map/ppermute | solution.py:22
  56.5 9.2 %collective-permute-start.3 = (f32[13,30,1,128]{3,1,2,0:T(8,128)S(1)}, f32[13,30,1,128]{3,1,2,0:T(8,128)S(1)}, u32[]{:S(2)}, u32[]{:S(2)}) collective-permute-start(f32[13,30,1,128]{3,1,2,0:T(8,128)S(1)} %get-tuple-element.29), channel_id=1, source_target_pairs={{32,0},{64,32},{96,64},{128,96},{160,128},{192,160},{224,192},{256... | collective-permute-start | bytes 599048 | tf_op jit(solution)/shard_map/ppermute | solution.py:23
  65.7 0.8 copy-start
  101.3 9.5 %collective-permute-start.4 = (f32[13,30,1,128]{3,1,2,0:T(8,128)S(1)}, f32[13,30,1,128]{3,1,2,0:T(8,128)S(1)}, u32[]{:S(2)}, u32[]{:S(2)}) collective-permute-start(f32[13,30,1,128]{3,1,2,0:T(8,128)S(1)} %get-tuple-element.24), channel_id=1, source_target_pairs={{0,32},{32,64},{64,96},{96,128},{128,160},{160,192},{192,224},{224... | collective-permute-start | bytes 599048 | tf_op jit(solution)/shard_map/ppermute | solution.py:22
  106.2 8.4 %collective-permute-start.5 = (f32[13,30,1,128]{3,1,2,0:T(8,128)S(1)}, f32[13,30,1,128]{3,1,2,0:T(8,128)S(1)}, u32[]{:S(2)}, u32[]{:S(2)}) collective-permute-start(f32[13,30,1,128]{3,1,2,0:T(8,128)S(1)} %get-tuple-element.25), channel_id=1, source_target_pairs={{32,0},{64,32},{96,64},{128,96},{160,128},{192,160},{224,192},{256... | collective-permute-start | bytes 599048 | tf_op jit(solution)/shard_map/ppermute | solution.py:23
  150.4 9.0 %collective-permute-start.6 = (f32[13,30,1,128]{3,1,2,0:T(8,128)S(1)}, f32[13,30,1,128]{3,1,2,0:T(8,128)S(1)}, u32[]{:S(2)}, u32[]{:S(2)}) collective-permute-start(f32[13,30,1,128]{3,1,2,0:T(8,128)S(1)} %get-tuple-element.20), channel_id=1, source_target_pairs={{0,32},{32,64},{64,96},{96,128},{128,160},{160,192},{192,224},{224... | collective-permute-start | bytes 599048 | tf_op jit(solution)/shard_map/ppermute | solution.py:22
  154.8 8.4 %collective-permute-start.7 = (f32[13,30,1,128]{3,1,2,0:T(8,128)S(1)}, f32[13,30,1,128]{3,1,2,0:T(8,128)S(1)}, u32[]{:S(2)}, u32[]{:S(2)}) collective-permute-start(f32[13,30,1,128]{3,1,2,0:T(8,128)S(1)} %get-tuple-element.21), channel_id=1, source_target_pairs={{32,0},{64,32},{96,64},{128,96},{160,128},{192,160},{224,192},{256... | collective-permute-start | bytes 599048 | tf_op jit(solution)/shard_map/ppermute | solution.py:23
